TPU v7x, 256 devices: a whole 4x4x8 slice. The times are simulated.
256 devices in a mesh: replica: 8 (over y, core), fsdp: 32 (over x, z).
Axes of the slice: x: 4, y: 4, z: 8, core: 2. Of those that a mesh axis runs over, the one named last changes fastest.
Arguments:
- anchor_params: bfloat16 [24, 512, 4096], P(None, 'fsdp')
- replica_params: bfloat16 [8, 24, 512, 4096], P('replica', None, 'fsdp')
- projection: bfloat16 [4096, 384], replicated
- momentum: float32 [24, 512, 384], P(None, 'fsdp'), may hold values from -1.8 to 1.8
- rate_table: float32 [4, 6], replicated, may hold values from 0.1 to 1
- owner_list: int32 [24], replicated, may hold values from 0 to 31, as said below
- layer_kind: int32 [24, 2], replicated, may hold values from 0 to 5, as said below
Outputs:
- new_params: bfloat16 [24, 512, 4096], P(None, 'fsdp')
- new_momentum: float32 [24, 512, 384], P(None, 'fsdp')
Inputs may be any that keep to these rules, and one draw needn't show every extreme that they name: `owner_list`: no fsdp index is named more than 2 times, and in every draw some index is named exactly 2 times. `layer_kind`: column 0 is a layer, column 1 a kind below 6; each layer has 6 rows, and no two rows are equal.
All inputs are finite; a program needn't handle non-finite values.
Results may differ from a plain program's by a relative error of at most 0.0055.
Values may be sent and summed in bfloat16 or wider, within the bound.
No kernel may reach another device: no remote copies, remote signals or barrier semaphores. Data moves between devices by JAX's collectives and lax.ppermute only.
A program may use at most 128 MiB of HBM per device.

v0:
```python
import jax
import jax.numpy as jnp
from jax import lax
from jax.experimental import pallas as pl
from jax.sharding import PartitionSpec as P


OUTER_MOMENTUM = 0.9
EPSILON = 1e-06


def apply_update(direction, projection_t, anchor, block=2048):
    rows, rank_dim = direction.shape
    model_width = projection_t.shape[1]

    def body(direction_ref, proj_ref, anchor_ref, out_ref):
        update = jnp.dot(direction_ref[...], proj_ref[...], preferred_element_type=jnp.float32)
        update = update.astype(jnp.bfloat16).astype(jnp.float32)
        out_ref[...] = (anchor_ref[...].astype(jnp.float32) - update).astype(jnp.bfloat16)

    return pl.pallas_call(
        body,
        grid=(model_width // block,),
        in_specs=[
            pl.BlockSpec((rows, rank_dim), lambda j: (0, 0)),
            pl.BlockSpec((rank_dim, block), lambda j: (0, j)),
            pl.BlockSpec((rows, block), lambda j: (0, j)),
        ],
        out_specs=pl.BlockSpec((rows, block), lambda j: (0, j)),
        out_shape=jax.ShapeDtypeStruct((rows, model_width), jnp.bfloat16),
    )(direction, projection_t, anchor)


def ring_steps(x, axis):
    even = [(0, 1), (2, 3)]
    odd = [(1, 2), (3, 0)]
    for step in range(2):
        perm = []
        for c in range(2):
            for a, b in (even if c == step else odd):
                perm += [(a * 2 + c, b * 2 + c), (b * 2 + c, a * 2 + c)]
        x = x + lax.ppermute(x, axis, perm)
    return x


def a2a_sum(v, axis):
    n = lax.axis_size(axis)
    return jnp.sum(lax.all_to_all(jnp.broadcast_to(v, (n,) + v.shape), axis, 0, 0, tiled=True), axis=0)


def local(anchor_params, replica_params, projection, momentum, rate_table, owner_list, layer_kind):
    matrices, rows_dev, model_width = anchor_params.shape
    rank_dim = projection.shape[1]
    all_rows = rows_dev * lax.axis_size("fsdp")
    n_replica = lax.axis_size("replica")
    highest = lax.Precision.HIGHEST
    half = matrices // 2
    core = lax.axis_index("replica") % 2
    swap = [(i, i ^ 1) for i in range(n_replica)]

    def compress(first):
        anchor = lax.dynamic_slice_in_dim(anchor_params, first, half)
        replica = lax.dynamic_slice_in_dim(replica_params[0], first, half)
        pseudo_grad = (anchor.astype(jnp.float32) - replica.astype(jnp.float32)).astype(jnp.bfloat16)
        return jnp.dot(
            pseudo_grad.reshape(half * rows_dev, model_width), projection, preferred_element_type=jnp.float32
        ).reshape(half, rows_dev, rank_dim)

    outgoing = lax.ppermute(compress((1 - core) * half), "replica", swap)
    own = ring_steps(lax.optimization_barrier(compress(core * half)) + outgoing, "replica")
    own_grad = own / n_replica
    own_momentum = OUTER_MOMENTUM * lax.dynamic_slice_in_dim(momentum, core * half, half) + own_grad
    own_step = own_grad + OUTER_MOMENTUM * own_momentum
    own_squares = a2a_sum(jnp.sum(own_step * own_step, axis=(1, 2)), "fsdp")
    other = lax.ppermute(own, "replica", swap)
    summed = jnp.where(core == 1, jnp.concatenate([other, own]), jnp.concatenate([own, other]))
    outer_grad = summed / n_replica
    new_momentum = OUTER_MOMENTUM * momentum + outer_grad
    outer_step = outer_grad + OUTER_MOMENTUM * new_momentum
    new_momentum, outer_step = lax.optimization_barrier((new_momentum, outer_step))
    other_squares = lax.ppermute(own_squares, "replica", swap)
    squares = jnp.where(
        core == 1,
        jnp.concatenate([other_squares, own_squares]),
        jnp.concatenate([own_squares, other_squares]),
    )
    same_group = (owner_list[:, None] == owner_list[None, :]).astype(jnp.float32)
    group_count = jnp.sum(same_group, axis=1)
    outer_rate = rate_table[layer_kind[:, 0], layer_kind[:, 1]]
    projection_t = projection.T
    group_squares = jnp.dot(same_group, squares, precision=highest)
    scaling = lax.rsqrt(group_squares / (group_count * (all_rows * rank_dim)) + EPSILON)
    direction = (outer_step * (outer_rate * scaling)[:, None, None]).astype(jnp.bfloat16)
    new_params = apply_update(
        direction.reshape(matrices * rows_dev, rank_dim),
        projection_t,
        anchor_params.reshape(matrices * rows_dev, model_width),
    ).reshape(matrices, rows_dev, model_width)
    return (new_params, new_momentum)


def solution(mesh):
    placed = (
        P(None, "fsdp", None),
        P("replica", None, "fsdp", None),
        P(),
        P(None, "fsdp", None),
        P(),
        P(),
        P(),
    )
    return jax.shard_map(
        local,
        mesh=mesh,
        in_specs=placed,
        out_specs=(P(None, "fsdp", None), P(None, "fsdp", None)),
        check_vma=False,
    )
```

profile of v0, /device:TPU:1, one launch (start us, length us, event | category | flops | bytes accessed | tf_op | source)
XLA Modules:
  0.0 56.0 jit_solution(1652285830826099234)
XLA Ops:
  0.6 0.0 copy-start
  0.7 0.0 copy-start.1
  0.7 4.7 %fusion.2 = f32[12,16,384]{2,1,0:T(8,128)} fusion(bf16[4096,384]{1,0:T(8,128)(2,1)} %param.9, bf16[1,24,16,4096]{3,2,1,0:T(8,128)(2,1)} %param.8, s32[]{:T(128)S(6)} %select_n.43, bf16[24,16,4096]{2,1,0:T(8,128)(2,1)} %param.7), kind=kOutput, calls=%fused_computation.5 | convolution fusion | flops 607125504 | bytes 6586372 | tf_op jit(solution)/shard_map/dot_general | solution.py:65
  5.4 3.2 %collective-permute-start = (f32[12,16,384]{2,1,0:T(8,128)}, f32[12,16,384]{2,1,0:T(8,128)S(1)}, u32[]{:S(2)}, u32[]{:S(2)}) collective-permute-start(f32[12,16,384]{2,1,0:T(8,128)} %fusion.2), channel_id=1, source_target_pairs={{0,32},{32,0},{64,96},{96,64},{128,160},{160,128},{192,224},{224,1... | collective-permute-start | bytes 884744 | tf_op jit(solution)/shard_map/ppermute | solution.py:69
  8.6 0.0 copy-done.1
  8.6 0.0 copy-start.3
  8.6 3.0 %fusion.4 = f32[12,16,384]{2,1,0:T(8,128)S(1)} fusion(bf16[4096,384]{1,0:T(8,128)(2,1)S(1)} %copy-done.1, bf16[1,24,16,4096]{3,2,1,0:T(8,128)(2,1)} %param.8, s32[]{:T(128)S(6)} %select_n.42, bf16[24,16,4096]{2,1,0:T(8,128)(2,1)} %param.7), kind=kOutput, calls=%fused_computation.7 | convolution fusion | flops 607125504 | bytes 6586372 | tf_op jit(solution)/shard_map/dot_general | solution.py:65
  11.6 0.0 collective-permute-done
  11.6 1.1 %collective-permute-start.1 = (f32[12,16,384]{2,1,0:T(8,128)S(1)}, f32[12,16,384]{2,1,0:T(8,128)S(1)}, u32[]{:S(2)}, u32[]{:S(2)}) collective-permute-start(f32[12,16,384]{2,1,0:T(8,128)S(1)} %add.48), channel_id=1, source_target_pairs={{0,64},{64,0},{128,192},{192,128},{96,160},{160,96},{224,32},{32,2... | collective-permute-start | bytes 884744 | tf_op jit(solution)/shard_map/ppermute | solution.py:42
  12.7 5.8 %collective-permute-done.1 = f32[12,16,384]{2,1,0:T(8,128)S(1)} collective-permute-done((f32[12,16,384]{2,1,0:T(8,128)S(1)}, f32[12,16,384]{2,1,0:T(8,128)S(1)}, u32[]{:S(2)}, u32[]{:S(2)}) %collective-permute-start.1) | collective-permute-done | bytes 294944 | tf_op jit(solution)/shard_map/ppermute | solution.py:42
  18.5 0.1 collective-permute-start.2
  18.6 0.0 copy-done.3
  18.7 5.8 %collective-permute-done.2 = f32[12,16,384]{2,1,0:T(8,128)S(1)} collective-permute-done((f32[12,16,384]{2,1,0:T(8,128)S(1)}, f32[12,16,384]{2,1,0:T(8,128)S(1)}, u32[]{:S(2)}, u32[]{:S(2)}) %collective-permute-start.2) | collective-permute-done | bytes 294944 | tf_op jit(solution)/shard_map/ppermute | solution.py:42
  24.5 0.0 copy-done.2
  24.5 0.2 multiply_reduce_fusion
  24.7 0.6 %broadcast_in_dim.2 = f32[32,1,12]{2,1,0:T(1,128)} broadcast(f32[12]{0:T(128)S(1)} %get-tuple-element.6), dimensions={2} | broadcast | bytes 1584 | tf_op jit(solution)/shard_map/broadcast_in_dim | solution.py:48
  25.3 9.4 %all-to-all-start = ((f32[32,1,12]{2,1,0:T(1,128)}), f32[32,1,12]{2,1,0:T(1,128)S(1)}, u32[]{:S(2)}, u32[]{:S(2)}) async-start(f32[32,1,12]{2,1,0:T(1,128)} %broadcast_in_dim.2), calls=%async_computation | async-start | bytes 32768 | tf_op jit(solution)/shard_map/all_to_all | solution.py:48
  34.7 2.3 %collective-permute-start.3 = (f32[12,16,384]{2,1,0:T(8,128)S(1)}, f32[12,16,384]{2,1,0:T(8,128)}, u32[]{:S(2)}, u32[]{:S(2)}) collective-permute-start(f32[12,16,384]{2,1,0:T(8,128)S(1)} %get-tuple-element.7), channel_id=1, source_target_pairs={{0,32},{32,0},{64,96},{96,64},{128,160},{160,128},{192,224},{224,1... | collective-permute-start | bytes 884744 | tf_op jit(solution)/shard_map/ppermute | solution.py:75
  37.0 0.0 copy-done.4
  37.0 0.2 fusion.20
  37.2 2.9 %copy.15 = bf16[4096,384]{0,1:T(8,128)(2,1)} copy(bf16[4096,384]{1,0:T(8,128)(2,1)S(1)} %copy-done.1) | data formatting | bytes 6291456 | tf_op args[2]
  40.1 0.0 copy-done
  40.1 0.8 %gather_fusion = f32[24]{0:T(128)S(1)} fusion(f32[4,6]{1,0:T(4,128)S(1)} %copy-done, s32[24]{0:T(128)S(1)} %fusion.38), kind=kCustom, calls=%fused_computation | custom fusion | bytes 384 | tf_op jit(solution)/shard_map/gather | solution.py:89
  41.0 2.3 %all-to-all-done = f32[32,1,12]{2,1,0:T(1,128)S(1)} async-done(((f32[32,1,12]{2,1,0:T(1,128)}), f32[32,1,12]{2,1,0:T(1,128)S(1)}, u32[]{:S(2)}, u32[]{:S(2)}) %all-to-all-start) | async-done | bytes 1568 | tf_op jit(solution)/shard_map/all_to_all | solution.py:48
  43.3 0.1 reduce_sum.28
  43.4 3.5 %collective-permute-start.4 = (f32[12]{0:T(128)S(1)}, f32[12]{0:T(128)S(1)}, u32[]{:S(2)}, u32[]{:S(2)}) collective-permute-start(f32[12]{0:T(128)S(1)} %reduce_sum.28), channel_id=1, source_target_pairs={{0,32},{32,0},{64,96},{96,64},{128,160},{160,128},{192,224},{224,1... | collective-permute-start | bytes 152 | tf_op jit(solution)/shard_map/ppermute | solution.py:81
  46.8 0.8 %collective-permute-done.4 = f32[12]{0:T(128)S(1)} collective-permute-done((f32[12]{0:T(128)S(1)}, f32[12]{0:T(128)S(1)}, u32[]{:S(2)}, u32[]{:S(2)}) %collective-permute-start.4) | collective-permute-done | bytes 80 | tf_op jit(solution)/shard_map/ppermute | solution.py:81
  47.6 0.2 fusion.17
  47.8 0.0 collective-permute-done.3
  47.8 2.2 %multiply_add_fusion = (f32[24,16,384]{2,1,0:T(8,128)S(1)}, f32[24,16,384]{2,1,0:T(8,128)}) fusion(f32[12,16,384]{2,1,0:T(8,128)} %collective-permute-done.3, f32[12,16,384]{2,1,0:T(8,128)S(1)} %get-tuple-element.7, pred[]{:T(512)S(6)} %eq.10, f32[24,16,384]{2,1,0:T(8,128)} %param.10), kind=kLoop, calls=%fused_computation.23 | loop fusion | flops 1179648 | bytes 2359297 | tf_op jit(solution)/shard_map/add | solution.py:79
  50.1 0.8 %multiply_convert_fusion = bf16[24,16,384]{2,1,0:T(8,128)(2,1)} fusion(f32[24,16,384]{2,1,0:T(8,128)S(1)} %get-tuple-element.4, f32[24]{0:T(128)S(1)} %fusion.17), kind=kLoop, calls=%fused_computation.22 | loop fusion | flops 294912 | bytes 884832 | tf_op jit(solution)/shard_map/convert_element_type | solution.py:93
  50.9 5.1 %shard_map.86 = bf16[384,4096]{1,0:T(8,128)(2,1)} custom-call(bf16[384,384]{1,0:T(8,128)(2,1)} %bitcast.39, bf16[384,4096]{1,0:T(8,128)(2,1)} %bitcast.36, bf16[384,4096]{1,0:T(8,128)(2,1)} %bitcast.37), custom_call_target="tpu_custom_call" | custom-call | tf_op jit(solution)/shard_map/pallas_call | solution.py:21
  (5 shorter events, 0.1 us)
Async XLA Ops:
  0.6 39.5 %copy-start = (f32[4,6]{1,0:T(4,128)S(1)}, f32[4,6]{1,0:T(4,128)}, u32[]{:S(2)}) copy-start(f32[4,6]{1,0:T(4,128)} %param.11) | copy-start | bytes 292
  0.7 7.9 %copy-start.1 = (bf16[4096,384]{1,0:T(8,128)(2,1)S(1)}, bf16[4096,384]{1,0:T(8,128)(2,1)}, u32[]{:S(2)}) copy-start(bf16[4096,384]{1,0:T(8,128)(2,1)} %param.9) | copy-start | bytes 9437188
  5.4 6.2 %collective-permute-start = (f32[12,16,384]{2,1,0:T(8,128)}, f32[12,16,384]{2,1,0:T(8,128)S(1)}, u32[]{:S(2)}, u32[]{:S(2)}) collective-permute-start(f32[12,16,384]{2,1,0:T(8,128)} %fusion.2), channel_id=1, source_target_pairs={{0,32},{32,0},{64,96},{96,64},{128,160},{160,128},{192,224},{224,1... | collective-permute-start | bytes 884744 | tf_op jit(solution)/shard_map/ppermute | solution.py:69
  8.6 10.1 %copy-start.3 = (s32[24,2]{0,1:T(2,128)S(1)}, s32[24,2]{0,1:T(2,128)}, u32[]{:S(2)}) copy-start(s32[24,2]{0,1:T(2,128)} %param.13) | copy-start | bytes 580
  8.6 15.9 %copy-start.2 = (f32[24,16,384]{2,1,0:T(8,128)S(1)}, f32[24,16,384]{2,1,0:T(8,128)}, u32[]{:S(2)}) copy-start(f32[24,16,384]{2,1,0:T(8,128)} %param.10) | copy-start | bytes 1769476
  8.6 28.5 %copy-start.4 = (s32[24]{0:T(128)S(1)}, s32[24]{0:T(128)}, u32[]{:S(2)}) copy-start(s32[24]{0:T(128)} %param.12) | copy-start | bytes 292
  11.6 6.9 %collective-permute-start.1 = (f32[12,16,384]{2,1,0:T(8,128)S(1)}, f32[12,16,384]{2,1,0:T(8,128)S(1)}, u32[]{:S(2)}, u32[]{:S(2)}) collective-permute-start(f32[12,16,384]{2,1,0:T(8,128)S(1)} %add.48), channel_id=1, source_target_pairs={{0,64},{64,0},{128,192},{192,128},{96,160},{160,96},{224,32},{32,2... | collective-permute-start | bytes 884744 | tf_op jit(solution)/shard_map/ppermute | solution.py:42
  18.5 6.0 %collective-permute-start.2 = (f32[12,16,384]{2,1,0:T(8,128)S(1)}, f32[12,16,384]{2,1,0:T(8,128)S(1)}, u32[]{:S(2)}, u32[]{:S(2)}) collective-permute-start(f32[12,16,384]{2,1,0:T(8,128)S(1)} %add.49), channel_id=1, source_target_pairs={{64,128},{128,64},{192,0},{0,192},{32,96},{96,32},{160,224},{224,1... | collective-permute-start | bytes 884744 | tf_op jit(solution)/shard_map/ppermute | solution.py:42
  25.3 18.0 %all-to-all-start = ((f32[32,1,12]{2,1,0:T(1,128)}), f32[32,1,12]{2,1,0:T(1,128)S(1)}, u32[]{:S(2)}, u32[]{:S(2)}) async-start(f32[32,1,12]{2,1,0:T(1,128)} %broadcast_in_dim.2), calls=%async_computation | async-start | bytes 32768 | tf_op jit(solution)/shard_map/all_to_all | solution.py:48
  34.7 13.1 %collective-permute-start.3 = (f32[12,16,384]{2,1,0:T(8,128)S(1)}, f32[12,16,384]{2,1,0:T(8,128)}, u32[]{:S(2)}, u32[]{:S(2)}) collective-permute-start(f32[12,16,384]{2,1,0:T(8,128)S(1)} %get-tuple-element.7), channel_id=1, source_target_pairs={{0,32},{32,0},{64,96},{96,64},{128,160},{160,128},{192,224},{224,1... | collective-permute-start | bytes 884744 | tf_op jit(solution)/shard_map/ppermute | solution.py:75
  43.4 4.3 %collective-permute-start.4 = (f32[12]{0:T(128)S(1)}, f32[12]{0:T(128)S(1)}, u32[]{:S(2)}, u32[]{:S(2)}) collective-permute-start(f32[12]{0:T(128)S(1)} %reduce_sum.28), channel_id=1, source_target_pairs={{0,32},{32,0},{64,96},{96,64},{128,160},{160,128},{192,224},{224,1... | collective-permute-start | bytes 152 | tf_op jit(solution)/shard_map/ppermute | solution.py:81
where the time goes:
time: 56.1 us; the launch traced here: 56 us
  starting transfers between devices  19.6 us (35%)
  waiting for transfers between devices  14.7 us (26%)
  matrix products  7.89 us (14%)
  Pallas kernels  5.05 us (9%)
  local copies, waits for them, and re-layouts  4.41 us (8%)
  other arithmetic  3.57 us (6%)
  between operations  0.73 us (1%)
    ppermute x2, waiting for transfers between devices, ring_steps(): x = x + lax.ppermute(x, axis, perm)  11.6 us
    all_to_all x1, starting transfers between devices, a2a_sum(): lax.all_to_all(jnp.broadcast_to(v, (n,) + v.shape), axis, 0, 0, tiled=True)  9.39 us
    dot_general x2, matrix products, compress(): jnp.dot(pseudo_grad.reshape(half * rows_dev, model_width), projection, pr...  7.69 us
    pallas_call x1, Pallas kernels, apply_update(): pl.pallas_call(body, grid=(model_width // block,), in_specs=[pl.BlockSpec...  5.05 us
    ppermute x1, starting transfers between devices, local(): other_squares = lax.ppermute(own_squares, 'replica', swap)  3.46 us
    ppermute x1, starting transfers between devices, local(): outgoing = lax.ppermute(compress((1 - core) * half), 'replica', swap)  3.2 us
    unnamed x11, local copies, waits for them, and re-layouts  2.95 us
    ppermute x1, starting transfers between devices, local(): other = lax.ppermute(own, 'replica', swap)  2.33 us
  transfers between devices with their start and end apart: 6, of which 4 were waited for; matrix products, arithmetic and copies ran while one was open for 13% of the time, Pallas kernels for 0%

commit v1 on v0

--- a/solution.py
+++ b/solution.py
@@ -2,6 +2,7 @@
 import jax.numpy as jnp
 from jax import lax
 from jax.experimental import pallas as pl
+from jax.experimental.pallas import tpu as pltpu
 from jax.sharding import PartitionSpec as P
 
 
@@ -9,11 +10,18 @@
 EPSILON = 1e-06
 
 
-def apply_update(direction, projection_t, anchor, block=2048):
-    rows, rank_dim = direction.shape
+def apply_update(outer_step, coef, projection_t, anchor, block=2048):
+    rows, rank_dim = outer_step.shape
     model_width = projection_t.shape[1]
+    per = rows // coef.shape[0]
 
-    def body(direction_ref, proj_ref, anchor_ref, out_ref):
+    def body(step_ref, coef_ref, proj_ref, anchor_ref, out_ref, direction_ref):
+        @pl.when(pl.program_id(0) == 0)
+        def _():
+            for m in range(coef.shape[0]):
+                part = step_ref[m * per:(m + 1) * per, :] * coef_ref[m]
+                direction_ref[m * per:(m + 1) * per, :] = part.astype(jnp.bfloat16)
+
         update = jnp.dot(direction_ref[...], proj_ref[...], preferred_element_type=jnp.float32)
         update = update.astype(jnp.bfloat16).astype(jnp.float32)
         out_ref[...] = (anchor_ref[...].astype(jnp.float32) - update).astype(jnp.bfloat16)
@@ -23,12 +31,14 @@
         grid=(model_width // block,),
         in_specs=[
             pl.BlockSpec((rows, rank_dim), lambda j: (0, 0)),
+            pl.BlockSpec(memory_space=pltpu.SMEM),
             pl.BlockSpec((rank_dim, block), lambda j: (0, j)),
             pl.BlockSpec((rows, block), lambda j: (0, j)),
         ],
         out_specs=pl.BlockSpec((rows, block), lambda j: (0, j)),
         out_shape=jax.ShapeDtypeStruct((rows, model_width), jnp.bfloat16),
-    )(direction, projection_t, anchor)
+        scratch_shapes=[pltpu.VMEM((rows, rank_dim), jnp.bfloat16)],
+    )(outer_step, coef, projection_t, anchor)
 
 
 def ring_steps(x, axis):
@@ -90,9 +100,9 @@
     projection_t = projection.T
     group_squares = jnp.dot(same_group, squares, precision=highest)
     scaling = lax.rsqrt(group_squares / (group_count * (all_rows * rank_dim)) + EPSILON)
-    direction = (outer_step * (outer_rate * scaling)[:, None, None]).astype(jnp.bfloat16)
     new_params = apply_update(
-        direction.reshape(matrices * rows_dev, rank_dim),
+        outer_step.reshape(matrices * rows_dev, rank_dim),
+        outer_rate * scaling,
         projection_t,
         anchor_params.reshape(matrices * rows_dev, model_width),
     ).reshape(matrices, rows_dev, model_width)

time: 56.1 us -> 55.5 us (0.989)
  other arithmetic: 3.57 us -> 1.65 us
  local copies, waits for them, and re-layouts: 4.41 us -> 6.25 us
  waiting for transfers between devices: 14.7 us -> 12.9 us
  matrix products: 7.89 us -> 8.92 us
    all_to_all x1, waiting for transfers between devices: 2.32 us -> 0.47 us  [a2a_sum(): lax.all_to_all(jnp.broadcast_to(v, (n,) + v.shape), axis, 0, 0, tiled=True)]
    unnamed x11 -> x13, local copies, waits for them, and re-layouts: 2.95 us -> 4.79 us
    add x1, other arithmetic: 2.24 us -> 1.14 us  [local(): outer_step = outer_grad + OUTER_MOMENTUM * new_momentum]
    convert_element_type x1 -> x0, other arithmetic: 0.82 us -> none  [local(): (outer_step * (outer_rate * scaling)[:, None, None]).astype(jnp.bfloat16)]
  transfers between devices with their start and end apart: 6 -> 6, of which waited for: 4 -> 4; matrix products, arithmetic and copies ran while one was open for 13% -> 18% of each run, Pallas kernels for 0% -> 0%
where the time goes in v1:
time: 55.5 us; the launch traced here: 55.3 us
  starting transfers between devices  19.6 us (35%)
  waiting for transfers between devices  12.9 us (23%)
  matrix products  8.92 us (16%)
  local copies, waits for them, and re-layouts  6.25 us (11%)
  Pallas kernels  5.23 us (9%)
  other arithmetic  1.65 us (3%)
  between operations  0.73 us (1%)
    ppermute x2, waiting for transfers between devices, ring_steps(): x = x + lax.ppermute(x, axis, perm)  11.6 us
    all_to_all x1, starting transfers between devices, a2a_sum(): lax.all_to_all(jnp.broadcast_to(v, (n,) + v.shape), axis, 0, 0, tiled=True)  9.39 us
    dot_general x2, matrix products, compress(): jnp.dot(pseudo_grad.reshape(half * rows_dev, model_width), projection, pr...  8.19 us
    pallas_call x1, Pallas kernels, apply_update(): pl.pallas_call(body, grid=(model_width // block,), in_specs=[pl.BlockSpec...  5.23 us
    unnamed x13, local copies, waits for them, and re-layouts  4.79 us
    ppermute x1, starting transfers between devices, local(): other_squares = lax.ppermute(own_squares, 'replica', swap)  3.47 us
    ppermute x1, starting transfers between devices, local(): outgoing = lax.ppermute(compress((1 - core) * half), 'replica', swap)  3.2 us
    ppermute x1, starting transfers between devices, local(): other = lax.ppermute(own, 'replica', swap)  2.33 us
  transfers between devices with their start and end apart: 6, of which 4 were waited for; matrix products, arithmetic and copies ran while one was open for 18% of the time, Pallas kernels for 0%

profile of v1, /device:TPU:1, one launch (start us, length us, event | category | flops | bytes accessed | tf_op | source)
XLA Modules:
  0.0 55.3 jit_solution(6411593438023112855)
XLA Ops:
  0.6 0.0 copy-start
  0.7 0.0 copy-start.1
  0.7 4.7 %fusion.2 = f32[12,16,384]{2,1,0:T(8,128)} fusion(bf16[4096,384]{1,0:T(8,128)(2,1)} %param.9, bf16[1,24,16,4096]{3,2,1,0:T(8,128)(2,1)} %param.8, s32[]{:T(128)S(6)} %select_n.43, bf16[24,16,4096]{2,1,0:T(8,128)(2,1)} %param.7), kind=kOutput, calls=%fused_computation.5 | convolution fusion | flops 607125504 | bytes 6586372 | tf_op jit(solution)/shard_map/dot_general | solution.py:75
  5.4 3.2 %collective-permute-start = (f32[12,16,384]{2,1,0:T(8,128)}, f32[12,16,384]{2,1,0:T(8,128)S(1)}, u32[]{:S(2)}, u32[]{:S(2)}) collective-permute-start(f32[12,16,384]{2,1,0:T(8,128)} %fusion.2), channel_id=1, source_target_pairs={{0,32},{32,0},{64,96},{96,64},{128,160},{160,128},{192,224},{224,1... | collective-permute-start | bytes 884744 | tf_op jit(solution)/shard_map/ppermute | solution.py:79
  8.6 0.0 copy-done.1
  8.6 3.5 %fusion.4 = f32[12,16,384]{2,1,0:T(8,128)S(1)} fusion(bf16[4096,384]{1,0:T(8,128)(2,1)} %param.9, bf16[1,24,16,4096]{3,2,1,0:T(8,128)(2,1)} %param.8, s32[]{:T(128)S(6)} %select_n.42, bf16[24,16,4096]{2,1,0:T(8,128)(2,1)S(1)} %copy-done.1), kind=kOutput, calls=%fused_computation.7 | convolution fusion | flops 607125504 | bytes 6586372 | tf_op jit(solution)/shard_map/dot_general | solution.py:75
  12.1 0.0 collective-permute-done
  12.1 1.1 %collective-permute-start.1 = (f32[12,16,384]{2,1,0:T(8,128)S(1)}, f32[12,16,384]{2,1,0:T(8,128)S(1)}, u32[]{:S(2)}, u32[]{:S(2)}) collective-permute-start(f32[12,16,384]{2,1,0:T(8,128)S(1)} %add.48), channel_id=1, source_target_pairs={{0,64},{64,0},{128,192},{192,128},{96,160},{160,96},{224,32},{32,2... | collective-permute-start | bytes 884744 | tf_op jit(solution)/shard_map/ppermute | solution.py:52
  13.3 5.8 %collective-permute-done.1 = f32[12,16,384]{2,1,0:T(8,128)S(1)} collective-permute-done((f32[12,16,384]{2,1,0:T(8,128)S(1)}, f32[12,16,384]{2,1,0:T(8,128)S(1)}, u32[]{:S(2)}, u32[]{:S(2)}) %collective-permute-start.1) | collective-permute-done | bytes 294944 | tf_op jit(solution)/shard_map/ppermute | solution.py:52
  19.0 0.1 collective-permute-start.2
  19.1 0.0 copy-done.4
  19.2 5.8 %collective-permute-done.2 = f32[12,16,384]{2,1,0:T(8,128)S(1)} collective-permute-done((f32[12,16,384]{2,1,0:T(8,128)S(1)}, f32[12,16,384]{2,1,0:T(8,128)S(1)}, u32[]{:S(2)}, u32[]{:S(2)}) %collective-permute-start.2) | collective-permute-done | bytes 294944 | tf_op jit(solution)/shard_map/ppermute | solution.py:52
  25.0 0.0 copy-done.2
  25.0 0.2 multiply_reduce_fusion
  25.2 0.6 %broadcast_in_dim.2 = f32[32,1,12]{2,1,0:T(1,128)} broadcast(f32[12]{0:T(128)S(1)} %get-tuple-element.6), dimensions={2} | broadcast | bytes 1584 | tf_op jit(solution)/shard_map/broadcast_in_dim | solution.py:58
  25.8 9.4 %all-to-all-start = ((f32[32,1,12]{2,1,0:T(1,128)}), f32[32,1,12]{2,1,0:T(1,128)S(1)}, u32[]{:S(2)}, u32[]{:S(2)}) async-start(f32[32,1,12]{2,1,0:T(1,128)} %broadcast_in_dim.2), calls=%async_computation | async-start | bytes 32768 | tf_op jit(solution)/shard_map/all_to_all | solution.py:58
  35.2 2.3 %collective-permute-start.3 = (f32[12,16,384]{2,1,0:T(8,128)S(1)}, f32[12,16,384]{2,1,0:T(8,128)S(1)}, u32[]{:S(2)}, u32[]{:S(2)}) collective-permute-start(f32[12,16,384]{2,1,0:T(8,128)S(1)} %get-tuple-element.7), channel_id=1, source_target_pairs={{0,32},{32,0},{64,96},{96,64},{128,160},{160,128},{192,224},{224,1... | collective-permute-start | bytes 884744 | tf_op jit(solution)/shard_map/ppermute | solution.py:85
  37.6 0.0 copy-done.5
  37.6 0.2 fusion.20
  37.7 0.0 copy-start.3
  37.7 4.8 %copy.15 = bf16[4096,384]{0,1:T(8,128)(2,1)} copy(bf16[4096,384]{1,0:T(8,128)(2,1)} %param.9) | data formatting | bytes 6291456 | tf_op args[2]
  42.5 0.0 copy-done
  42.5 0.8 %gather_fusion = f32[24]{0:T(128)S(1)} fusion(f32[4,6]{1,0:T(4,128)S(1)} %copy-done, s32[24]{0:T(128)S(1)} %fusion.38), kind=kCustom, calls=%fused_computation | custom fusion | bytes 384 | tf_op jit(solution)/shard_map/gather | solution.py:99
  43.3 0.5 all-to-all-done
  43.8 0.1 reduce_sum.28
  43.9 3.5 %collective-permute-start.4 = (f32[12]{0:T(128)S(1)}, f32[12]{0:T(128)S(1)}, u32[]{:S(2)}, u32[]{:S(2)}) collective-permute-start(f32[12]{0:T(128)S(1)} %reduce_sum.28), channel_id=1, source_target_pairs={{0,32},{32,0},{64,96},{96,64},{128,160},{160,128},{192,224},{224,1... | collective-permute-start | bytes 152 | tf_op jit(solution)/shard_map/ppermute | solution.py:91
  47.3 0.8 %collective-permute-done.4 = f32[12]{0:T(128)S(1)} collective-permute-done((f32[12]{0:T(128)S(1)}, f32[12]{0:T(128)S(1)}, u32[]{:S(2)}, u32[]{:S(2)}) %collective-permute-start.4) | collective-permute-done | bytes 80 | tf_op jit(solution)/shard_map/ppermute | solution.py:91
  48.2 0.7 %fusion.17.coef_ref = f32[24]{0:T(128)} fusion(f32[24]{0:T(128)S(1)} %gather_fusion, s32[24]{0:T(128)S(1)} %copy-done.5, pred[]{:T(512)S(6)} %eq.10, f32[12]{0:T(128)S(1)} %reduce_sum.28, f32[12]{0:T(128)S(1)} %collective-permute-done.4, f32[24]{0:T(128)S(1)} %fusion.20), kind=kOutput, calls=%fused_computation.19 | convolution fusion | flops 7656 | bytes 481 | tf_op jit(solution)/shard_map/dot_general | solution.py:101
  48.9 0.0 collective-permute-done.3
  48.9 0.0 copy-done.3
  48.9 1.1 %multiply_add_fusion = (f32[24,16,384]{2,1,0:T(8,128)}, f32[24,16,384]{2,1,0:T(8,128)}) fusion(f32[12,16,384]{2,1,0:T(8,128)S(1)} %collective-permute-done.3, f32[12,16,384]{2,1,0:T(8,128)S(1)} %get-tuple-element.7, pred[]{:T(512)S(6)} %eq.10, f32[24,16,384]{2,1,0:T(8,128)S(1)} %copy-done.3), kind=kLoop, calls=%fused_computation.22 | loop fusion | flops 1179648 | bytes 2359297 | tf_op jit(solution)/shard_map/add | solution.py:89
  50.0 5.2 %shard_map.86 = bf16[384,4096]{1,0:T(8,128)(2,1)} custom-call(f32[384,384]{1,0:T(8,128)} %bitcast.39, f32[24]{0:T(128)} %fusion.17.coef_ref, bf16[384,4096]{1,0:T(8,128)(2,1)} %bitcast.36, bf16[384,4096]{1,0:T(8,128)(2,1)} %bitcast.37), custom_call_target="tpu_custom_call" | custom-call | tf_op jit(solution)/shard_map/pallas_call | solution.py:29
  (6 shorter events, 0.1 us)
Async XLA Ops:
  0.6 41.9 %copy-start = (f32[4,6]{1,0:T(4,128)S(1)}, f32[4,6]{1,0:T(4,128)}, u32[]{:S(2)}) copy-start(f32[4,6]{1,0:T(4,128)} %param.11) | copy-start | bytes 292
  0.7 7.9 %copy-start.1 = (bf16[24,16,4096]{2,1,0:T(8,128)(2,1)S(1)}, bf16[24,16,4096]{2,1,0:T(8,128)(2,1)}, u32[]{:S(2)}) copy-start(bf16[24,16,4096]{2,1,0:T(8,128)(2,1)} %param.7) | copy-start | bytes 9437188
  5.4 6.7 %collective-permute-start = (f32[12,16,384]{2,1,0:T(8,128)}, f32[12,16,384]{2,1,0:T(8,128)S(1)}, u32[]{:S(2)}, u32[]{:S(2)}) collective-permute-start(f32[12,16,384]{2,1,0:T(8,128)} %fusion.2), channel_id=1, source_target_pairs={{0,32},{32,0},{64,96},{96,64},{128,160},{160,128},{192,224},{224,1... | collective-permute-start | bytes 884744 | tf_op jit(solution)/shard_map/ppermute | solution.py:79
  8.6 10.6 %copy-start.4 = (s32[24,2]{0,1:T(2,128)S(1)}, s32[24,2]{0,1:T(2,128)}, u32[]{:S(2)}) copy-start(s32[24,2]{0,1:T(2,128)} %param.13) | copy-start | bytes 580
  8.6 16.4 %copy-start.2 = (f32[24,16,384]{2,1,0:T(8,128)S(1)}, f32[24,16,384]{2,1,0:T(8,128)}, u32[]{:S(2)}) copy-start(f32[24,16,384]{2,1,0:T(8,128)} %param.10) | copy-start | bytes 1769476
  8.6 29.0 %copy-start.5 = (s32[24]{0:T(128)S(1)}, s32[24]{0:T(128)}, u32[]{:S(2)}) copy-start(s32[24]{0:T(128)} %param.12) | copy-start | bytes 292
  12.1 6.9 %collective-permute-start.1 = (f32[12,16,384]{2,1,0:T(8,128)S(1)}, f32[12,16,384]{2,1,0:T(8,128)S(1)}, u32[]{:S(2)}, u32[]{:S(2)}) collective-permute-start(f32[12,16,384]{2,1,0:T(8,128)S(1)} %add.48), channel_id=1, source_target_pairs={{0,64},{64,0},{128,192},{192,128},{96,160},{160,96},{224,32},{32,2... | collective-permute-start | bytes 884744 | tf_op jit(solution)/shard_map/ppermute | solution.py:52
  19.0 6.0 %collective-permute-start.2 = (f32[12,16,384]{2,1,0:T(8,128)S(1)}, f32[12,16,384]{2,1,0:T(8,128)S(1)}, u32[]{:S(2)}, u32[]{:S(2)}) collective-permute-start(f32[12,16,384]{2,1,0:T(8,128)S(1)} %add.49), channel_id=1, source_target_pairs={{64,128},{128,64},{192,0},{0,192},{32,96},{96,32},{160,224},{224,1... | collective-permute-start | bytes 884744 | tf_op jit(solution)/shard_map/ppermute | solution.py:52
  25.8 18.0 %all-to-all-start = ((f32[32,1,12]{2,1,0:T(1,128)}), f32[32,1,12]{2,1,0:T(1,128)S(1)}, u32[]{:S(2)}, u32[]{:S(2)}) async-start(f32[32,1,12]{2,1,0:T(1,128)} %broadcast_in_dim.2), calls=%async_computation | async-start | bytes 32768 | tf_op jit(solution)/shard_map/all_to_all | solution.py:58
  35.2 13.7 %collective-permute-start.3 = (f32[12,16,384]{2,1,0:T(8,128)S(1)}, f32[12,16,384]{2,1,0:T(8,128)S(1)}, u32[]{:S(2)}, u32[]{:S(2)}) collective-permute-start(f32[12,16,384]{2,1,0:T(8,128)S(1)} %get-tuple-element.7), channel_id=1, source_target_pairs={{0,32},{32,0},{64,96},{96,64},{128,160},{160,128},{192,224},{224,1... | collective-permute-start | bytes 884744 | tf_op jit(solution)/shard_map/ppermute | solution.py:85
  37.7 11.2 %copy-start.3 = (f32[24,16,384]{2,1,0:T(8,128)S(1)}, f32[24,16,384]{2,1,0:T(8,128)}, u32[]{:S(2)}) copy-start(f32[24,16,384]{2,1,0:T(8,128)} %param.10) | copy-start | bytes 1769476
  43.9 4.3 %collective-permute-start.4 = (f32[12]{0:T(128)S(1)}, f32[12]{0:T(128)S(1)}, u32[]{:S(2)}, u32[]{:S(2)}) collective-permute-start(f32[12]{0:T(128)S(1)} %reduce_sum.28), channel_id=1, source_target_pairs={{0,32},{32,0},{64,96},{96,64},{128,160},{160,128},{192,224},{224,1... | collective-permute-start | bytes 152 | tf_op jit(solution)/shard_map/ppermute | solution.py:91
